TPU v7x, 256 devices: a whole 4x4x8 slice. The times are simulated.
256 devices in a mesh: dp: 16 (over y_hi, z), ctx: 4 (over y_lo, core), uly: 4 (over x).
Axes of the slice: x: 4, y: 4 (y_hi: 2, y_lo: 2; y = y_hi * 2 + y_lo), z: 8, core: 2. Of those that a mesh axis runs over, the one named last changes fastest.
Arguments:
- queries: bfloat16 [16, 3072, 1536], P('dp', ('ctx', 'uly')), may hold values from -4.5 to 4.5
- key_rows: bfloat16 [16, 3072, 1536], P('dp', ('ctx', 'uly')), may hold values from -4.5 to 4.5
- value_rows: bfloat16 [16, 3072, 1536], P('dp', ('ctx', 'uly')), may hold values from -5 to 5
- out_grad: bfloat16 [16, 3072, 3072], P('dp', 'ctx'), may hold values from -6 to 6
- out_weight: bfloat16 [1536, 3072], P('uly'), may hold values from -0.15625 to 0.15625
- tile_lists: int32 [8, 6], replicated, may hold values from -1 to 7, as said below
- windows: int32 [12, 2], replicated, may hold values from 0 to 1, as said below
Outputs:
- query_grad: bfloat16 [16, 3072, 1536], P('dp', ('ctx', 'uly'))
- key_grad: bfloat16 [16, 3072, 1536], P('dp', ('ctx', 'uly'))
- value_grad: bfloat16 [16, 3072, 1536], P('dp', ('ctx', 'uly'))
- weight_grad: bfloat16 [1536, 3072], P('uly')
Inputs may be any that keep to these rules, and one draw needn't show every extreme that they name: `tile_lists`: entry j of row Q = f * 2 + s is -1 or (f + j // 2 - 1) * 2 + j % 2; it is -1 wherever f + j // 2 - 1 lies outside 0 to 3, and never at an in-range entry with j % 2 == s. Of any two consecutive heads, at least one has windows[h, 0] = 1.
All inputs are finite; a program needn't handle non-finite values.
Results may differ from a plain program's by a relative error of at most 0.014.
Values may be sent and summed in bfloat16 or wider, within the bound.
No kernel may reach another device: no remote copies, remote signals or barrier semaphores. Data moves between devices by JAX's collectives and lax.ppermute only.
A program may use at most 192 MiB of HBM per device.

v0:
```python
import jax
import jax.numpy as jnp
from jax import lax
from jax.sharding import PartitionSpec as P

HEADS = 12
HD = 128
TILE = 384
TW = 2
FT_DEV = 1


def extended(x, sides, width):
    for axis, dim in sides:
        count, length = (lax.axis_size(axis), x.shape[dim])
        up = [(i, (i + 1) % count) for i in range(count - 1)]
        down = [(j, i) for i, j in up]
        last = lax.slice_in_dim(x, length - width, length, axis=dim)
        initial = lax.slice_in_dim(x, 0, width, axis=dim)
        before = lax.ppermute(last, axis, up)
        after = lax.ppermute(initial, axis, down)
        x = jnp.concatenate([before, x, after], axis=dim)
    return x


def cross_rounded(parts):
    lowered = lax.optimization_barrier(parts.astype(jnp.bfloat16)).astype(jnp.float32)
    return jnp.concatenate([lowered[0:1], parts[1:2], lowered[2:3]], axis=0)


def score_grid_of(query_tile, key_window):
    scaling = HD ** (-0.5)
    scores = jnp.dot(query_tile, key_window.T, preferred_element_type=jnp.float32) * scaling
    return scores.reshape(TW, TILE, 3 * TW, TILE)


def forward_block(query_tile, key_window, value_window, allow):
    score_grid = score_grid_of(query_tile, key_window)
    key_mask = allow[:, None, :, None]
    row_max = jnp.max(jnp.where(key_mask, score_grid, -jnp.inf), axis=(2, 3), keepdims=True)
    raised = jnp.where(key_mask, jnp.exp(score_grid - row_max), 0.0)
    totals = jnp.sum(raised, axis=(2, 3), keepdims=True)
    mixing = (raised / totals).reshape(TW * TILE, 3 * TW * TILE)
    out_low = jnp.dot(
        mixing.astype(jnp.bfloat16), value_window, preferred_element_type=jnp.float32
    ).astype(jnp.bfloat16)
    return (mixing, out_low, row_max, totals)


def backward_block(query_tile, key_window, value_window, grad_tile, mixing, out_low):
    scaling = HD ** (-0.5)
    mixing_low = mixing.astype(jnp.bfloat16)
    row_delta = jnp.sum(
        out_low.astype(jnp.float32) * grad_tile.astype(jnp.float32), axis=1, keepdims=True
    )
    value_part = lax.dot_general(
        mixing_low, grad_tile, (((0,), (0,)), ((), ())), preferred_element_type=jnp.float32
    )
    prob_grad = jnp.dot(grad_tile, value_window.T, preferred_element_type=jnp.float32)
    score_grad = (mixing * (prob_grad - row_delta) * scaling).astype(jnp.bfloat16)
    query_part = jnp.dot(score_grad, key_window, preferred_element_type=jnp.float32)
    key_part = lax.dot_general(
        score_grad, query_tile, (((0,), (0,)), ((), ())), preferred_element_type=jnp.float32
    )
    return (query_part, key_part, value_part)


def weight_sum(attended, token_grads):
    local_term = lax.dot_general(
        attended, token_grads, (((0,), (0,)), ((), ())), preferred_element_type=jnp.float32
    )
    grand_total = lax.psum(local_term, ("dp", "ctx"))
    return (grand_total / lax.axis_size("dp")).astype(jnp.bfloat16)


def on_device(queries, key_rows, value_rows, out_grad, out_weight, tile_lists, windows):
    heads_here = HEADS // lax.axis_size("uly")
    width_here = heads_here * HD
    layer_rows = TW * TILE
    span_rows = FT_DEV * layer_rows
    query_heads, pair_heads = (
        lax.all_to_all(queries[None], "uly", split_axis=3, concat_axis=2, tiled=True),
        lax.all_to_all(
            jnp.stack([key_rows, value_rows]), "uly", split_axis=3, concat_axis=2, tiled=True
        ),
    )
    query_heads = query_heads.reshape(FT_DEV, layer_rows, heads_here, HD)
    window = extended(pair_heads, (("ctx", 1),), 1)
    window = window.reshape(2, FT_DEV + 2, layer_rows, heads_here, HD)
    grad_out = lax.dot_general(
        out_grad[0], out_weight, (((1,), (1,)), ((), ())), preferred_element_type=jnp.float32
    )
    grad_out = grad_out.astype(jnp.bfloat16).reshape(FT_DEV, layer_rows, heads_here, HD)
    ctx_at = lax.axis_index("ctx")
    uly_at = lax.axis_index("uly")
    list_rows = lax.dynamic_slice_in_dim(tile_lists, ctx_at * (FT_DEV * TW), FT_DEV * TW, 0)
    listed = (list_rows >= 0).reshape(FT_DEV, TW, 3 * TW)
    reach_rows = lax.dynamic_slice_in_dim(windows, uly_at * heads_here, heads_here, 0)
    slot_ids = jnp.arange(3 * TW, dtype=jnp.int32)
    slot_time = slot_ids // TW - 1
    slot_space = slot_ids % TW
    spot_ids = jnp.arange(TW, dtype=jnp.int32)
    near_time = jnp.abs(slot_time)[None, :] <= reach_rows[:, 0:1]
    near_space = (
        jnp.abs(slot_space[None, :] - spot_ids[:, None])[None, :, :]
        <= reach_rows[:, 1][:, None, None]
    )
    allowed = listed[:, None, :, :] & near_time[None, :, None, :] & near_space[None, :, :, :]

    def tiles_of(frame_at, head_at):
        query_tile = query_heads[frame_at, :, head_at]
        key_window = window[0, frame_at : frame_at + 3, :, head_at].reshape(3 * layer_rows, HD)
        value_window = window[1, frame_at : frame_at + 3, :, head_at].reshape(3 * layer_rows, HD)
        return (query_tile, key_window, value_window)

    def assemble(per_block):
        frames_list = [jnp.stack(per_block[0], axis=1)]
        return jnp.stack(frames_list, axis=0).reshape(span_rows, width_here)

    pair_total = jnp.zeros((2, FT_DEV + 2, layer_rows, heads_here, HD), jnp.float32)
    out_blocks = [[None] * heads_here]
    query_blocks = [[None] * heads_here]

    def add_back(pair_total, frame_at, head_at, mixing, out_low):
        query_tile, key_window, value_window = tiles_of(frame_at, head_at)
        query_part, key_part, value_part = backward_block(
            query_tile, key_window, value_window, grad_out[frame_at, :, head_at], mixing, out_low
        )
        query_blocks[frame_at][head_at] = query_part.astype(jnp.bfloat16)
        pair_total = pair_total.at[0, frame_at : frame_at + 3, :, head_at].add(
            cross_rounded(key_part.reshape(3, layer_rows, HD))
        )
        pair_total = pair_total.at[1, frame_at : frame_at + 3, :, head_at].add(
            cross_rounded(value_part.reshape(3, layer_rows, HD))
        )
        return pair_total

    frame_at = 0
    for head_at in range(heads_here):
        query_tile, key_window, value_window = tiles_of(frame_at, head_at)
        mixing, out_low, row_max, totals = forward_block(
            query_tile, key_window, value_window, allowed[frame_at, head_at]
        )
        out_blocks[frame_at][head_at] = out_low
        pair_total = add_back(pair_total, frame_at, head_at, mixing, out_low)
    attended = assemble(out_blocks)
    weight_grad = weight_sum(attended, out_grad[0])
    outgoing = jnp.stack([pair_total[:, 0], pair_total[:, FT_DEV + 1]]).astype(jnp.bfloat16)
    returned = extended(outgoing, (("ctx", 0),), 1).astype(jnp.float32)
    own_grads = pair_total[:, 1 : FT_DEV + 1]
    own_grads = own_grads.at[:, 0].add(returned[0])
    own_grads = own_grads.at[:, FT_DEV - 1].add(returned[3])
    key_heads = own_grads[0].reshape(1, span_rows, width_here).astype(jnp.bfloat16)
    value_heads = own_grads[1].reshape(1, span_rows, width_here).astype(jnp.bfloat16)
    query_grad_heads = assemble(query_blocks).reshape(1, span_rows, width_here)
    tokens_back = (
        lax.all_to_all(query_grad_heads, "uly", split_axis=1, concat_axis=2, tiled=True),
        lax.all_to_all(key_heads, "uly", split_axis=1, concat_axis=2, tiled=True),
        lax.all_to_all(value_heads, "uly", split_axis=1, concat_axis=2, tiled=True),
    )
    return (tokens_back[0], tokens_back[1], tokens_back[2], weight_grad)


def solution(mesh):
    in_specs = (
        P("dp", ("ctx", "uly"), None),
        P("dp", ("ctx", "uly"), None),
        P("dp", ("ctx", "uly"), None),
        P("dp", "ctx", None),
        P("uly", None),
        P(),
        P(),
    )
    out_specs = (
        P("dp", ("ctx", "uly"), None),
        P("dp", ("ctx", "uly"), None),
        P("dp", ("ctx", "uly"), None),
        P("uly", None),
    )
    return jax.shard_map(
        on_device, mesh=mesh, in_specs=in_specs, out_specs=out_specs, check_vma=False
    )
```

profile of v0, /device:TPU:2, one launch (start us, length us, event | category | flops | bytes accessed | tf_op | source)
XLA Modules:
  0.0 417.1 jit_solution(2626870744510376897)
XLA Ops:
  8.7 2.9 copy.189
  11.6 6.7 %all-to-all-start = ((bf16[2,1,192,1536]{2,0,1,3:T(2,128)(2,1)}), bf16[2,1,192,1536]{2,0,1,3:T(2,128)(2,1)}, u32[]{:S(2)}, u32[]{:S(2)}) async-start(bf16[2,1,192,1536]{2,0,1,3:T(2,128)(2,1)} %copy.189), calls=%async_computation | async-start | bytes 3145728 | tf_op jit(solution)/shard_map/all_to_all | solution.py:83
  18.3 2.9 copy.197
  21.8 9.9 %reduce.34 = bf16[1536,192]{1,0:T(8,128)(2,1)S(1)} reduce(bf16[1536,1,1,192]{3,2,1,0:T(2,128)(2,1)} %bitcast.304, bf16[]{:T(256)} %broadcast.396), dimensions={1,2}, to_apply=%bitcast.238.reduce_sub_computation | reduce | bytes 1179650
  36.0 5.5 %all-to-all-start.1 = ((bf16[4,2,36864]{2,1,0:T(2,128)(2,1)}), bf16[4,2,36864]{2,1,0:T(2,128)(2,1)}, u32[]{:S(2)}, u32[]{:S(2)}) async-start(bf16[4,2,36864]{2,1,0:T(2,128)(2,1)} %reshape.571), calls=%async_computation.1 | async-start | bytes 1179648 | tf_op jit(solution)/shard_map/all_to_all | solution.py:82
  41.5 4.3 %copy.237 = bf16[2,1,192,4,384]{4,3,2,0,1:T(4,128)(2,1)S(1)} copy(bf16[2,1,192,4,384]{2,0,4,3,1:T(2,128)(2,1)} %bitcast.5) | data formatting | bytes 2359296 | tf_op jit(solution)/shard_map/all_to_all | solution.py:83
  48.3 4.6 %collective-permute-start = (bf16[2,1,768,384]{3,2,0,1:T(8,128)(2,1)}, bf16[2,1,768,384]{3,2,0,1:T(8,128)(2,1)}, u32[]{:S(2)}, u32[]{:S(2)}) collective-permute-start(bf16[2,1,768,384]{3,2,0,1:T(8,128)(2,1)} %bitcast.7), channel_id=1, source_target_pairs={{0,4},{4,8},{8,12},{1,5},{5,9},{9,13},{2,6},{6,10},{10,14},{3,7},{... | collective-permute-start | bytes 3538952 | tf_op jit(solution)/shard_map/ppermute | solution.py:20
  55.2 3.3 copy.206
  60.0 3.2 copy.211
  64.7 3.2 copy.201
  71.3 5.4 %fusion.34 = bf16[768,384]{0,1:T(8,128)(2,1)} fusion(bf16[384,3072]{1,0:T(8,128)(2,1)S(1)} %copy-done, bf16[1,768,3072]{2,1,0:T(8,128)(2,1)} %param.26), kind=kOutput, calls=%fused_computation.50 | convolution fusion | flops 1812234240 | bytes 7667712 | tf_op jit(solution)/shard_map/dot_general | solution.py:90
  105.6 4.5 %fusion.92 = (bf16[2304,128]{0,1:T(8,128)(2,1)S(1)}, f32[2304,128]{0,1:T(8,128)}) fusion(bf16[1,768,3,128]{1,3,2,0:T(8,128)(2,1)} %bitcast.355, f32[768]{0:T(1024)S(1)} %fusion.14, pred[768,2304]{0,1:T(32,128)(4,1)S(1)} %copy-done.7, f32[768]{0:T(1024)S(1)} %get-tuple-element.137, f32[2304,768]{1,0:T(8,128)S(1)} %get-tuple-element.138), kind=kOutput, calls=%fused_computation.143 | convolution fusion | flops 462127104 | bytes 10819584 | tf_op jit(solution)/shard_map/dot_general | solution.py:56
  119.6 4.8 %fusion.96 = (bf16[2304,128]{0,1:T(8,128)(2,1)S(1)}, f32[2304,128]{0,1:T(8,128)}) fusion(bf16[1,768,3,128]{1,3,2,0:T(8,128)(2,1)} %bitcast.356, f32[768]{0:T(1024)S(1)} %fusion.18, pred[768,2304]{0,1:T(32,128)(4,1)S(1)} %copy-done.9, f32[768]{0:T(1024)S(1)} %get-tuple-element.139, f32[2304,768]{1,0:T(8,128)S(1)} %get-tuple-element.140), kind=kOutput, calls=%fused_computation.147 | convolution fusion | flops 462127104 | bytes 10819584 | tf_op jit(solution)/shard_map/dot_general | solution.py:56
  124.4 3.2 fusion.48
  136.9 3.5 fusion.94
  140.5 3.0 fusion.45
  143.6 3.8 multiply_reduce_fusion.2
  147.4 3.0 multiply_convert_fusion
  153.0 3.0 multiply_convert_fusion.2
  171.5 5.1 %multiply_convert_fusion.1 = bf16[768,2304]{0,1:T(8,128)(2,1)S(1)} fusion(bf16[2304,128]{1,0:T(8,128)(2,1)S(1)} %bitcast.336, f32[768]{0:T(1024)S(1)} %copy-done.53, bf16[1,768,3,128]{1,3,2,0:T(8,128)(2,1)} %bitcast.357, f32[768]{0:T(1024)S(1)} %copy-done.45, pred[768,2304]{0,1:T(32,128)(4,1)S(1)} %copy-done.6, f32[768]{0:T(1024)S(1)} %get-tuple-element.141, ...), kind=kOutput, calls=%fused_computation.16 | convolution fusion | flops 467140608 | bytes 13181952 | tf_op jit(solution)/shard_map/dot_general | solution.py:59
  195.9 3.3 collective-permute-start.2
  200.6 4.1 fusion.9
  204.8 2.8 fusion.53
  211.4 4.2 %reduce.35 = bf16[768,384]{1,0:T(8,128)(2,1)S(1)} reduce(bf16[768,1,384]{2,1,0:T(2,128)(2,1)S(1)} %bitcast.316, bf16[]{:T(256)} %broadcast.396), dimensions={1}, to_apply=%bitcast.240.reduce_sub_computation | reduce | bytes 1179650
  216.6 4.8 %all-to-all-start.2 = ((bf16[4,2,36864]{2,1,0:T(2,128)(2,1)}), bf16[4,2,36864]{2,1,0:T(2,128)(2,1)S(1)}, u32[]{:S(2)}, u32[]{:S(2)}) async-start(bf16[4,2,36864]{2,1,0:T(2,128)(2,1)} %reshape.573), calls=%async_computation.2 | async-start | bytes 1179648 | tf_op jit(solution)/shard_map/all_to_all | solution.py:157
  225.4 4.2 %reduce.36 = bf16[768,384]{1,0:T(8,128)(2,1)S(1)} reduce(bf16[768,1,384]{2,1,0:T(2,128)(2,1)S(1)} %bitcast.317, bf16[]{:T(256)} %broadcast.396), dimensions={1}, to_apply=%bitcast.242.reduce_sub_computation | reduce | bytes 1179650
  231.4 5.2 %all-to-all-start.3 = ((bf16[4,2,36864]{2,1,0:T(2,128)(2,1)}), bf16[4,2,36864]{2,1,0:T(2,128)(2,1)S(1)}, u32[]{:S(2)}, u32[]{:S(2)}) async-start(bf16[4,2,36864]{2,1,0:T(2,128)(2,1)} %reshape.575), calls=%async_computation.3 | async-start | bytes 1179648 | tf_op jit(solution)/shard_map/all_to_all | solution.py:158
  237.9 4.2 %reduce.37 = bf16[768,384]{1,0:T(8,128)(2,1)S(1)} reduce(bf16[768,1,384]{2,1,0:T(2,128)(2,1)S(1)} %bitcast.315, bf16[]{:T(256)} %broadcast.396), dimensions={1}, to_apply=%bitcast.244.reduce_sub_computation | reduce | bytes 1179650
  245.8 4.9 %all-to-all-start.4 = ((bf16[4,2,36864]{2,1,0:T(2,128)(2,1)}), bf16[4,2,36864]{2,1,0:T(2,128)(2,1)S(1)}, u32[]{:S(2)}, u32[]{:S(2)}) async-start(bf16[4,2,36864]{2,1,0:T(2,128)(2,1)} %reshape.577), calls=%async_computation.4 | async-start | bytes 1179648 | tf_op jit(solution)/shard_map/all_to_all | solution.py:159
  253.8 5.3 %all-to-all-done.4 = bf16[4,2,36864]{2,1,0:T(2,128)(2,1)S(1)} async-done(((bf16[4,2,36864]{2,1,0:T(2,128)(2,1)}), bf16[4,2,36864]{2,1,0:T(2,128)(2,1)S(1)}, u32[]{:S(2)}, u32[]{:S(2)}) %all-to-all-start.4) | async-done | bytes 589856 | tf_op jit(solution)/shard_map/all_to_all | solution.py:159
  260.6 145.3 %all-reduce.3.cloned.1.call-done = f32[384,3072]{1,0:T(8,128)} async-done(((f32[384,3072]{1,0:T(8,128)}), f32[384,3072]{1,0:T(8,128)}) %all-reduce.3.cloned.1.call-update) | async-done | bytes 4718608 | tf_op jit(solution)/shard_map/psum | solution.py:72
  405.9 4.1 multiply_convert_fusion.3
  (242 shorter events, 123.7 us)
Async XLA Ops:
  7.2 64.1 %copy-start = (bf16[384,3072]{1,0:T(8,128)(2,1)S(1)}, bf16[384,3072]{1,0:T(8,128)(2,1)}, u32[]{:S(2)}) copy-start(bf16[384,3072]{1,0:T(8,128)(2,1)} %param.27) | copy-start | bytes 7077892
  8.7 9.6 %copy-start.50 = (s32[12,2]{0,1:T(2,128)S(1)}, s32[12,2]{0,1:T(2,128)}, u32[]{:S(2)}) copy-start(s32[12,2]{0,1:T(2,128)} %param.29) | copy-start | bytes 292
  11.6 6.8 %copy-start.38 = (bf16[1,192,1536]{2,1,0:T(8,128)(2,1)S(1)}, bf16[1,192,1536]{2,1,0:T(8,128)(2,1)}, u32[]{:S(2)}) copy-start(bf16[1,192,1536]{2,1,0:T(8,128)(2,1)} %param.23) | copy-start | bytes 1769476
  11.6 24.4 %all-to-all-start = ((bf16[2,1,192,1536]{2,0,1,3:T(2,128)(2,1)}), bf16[2,1,192,1536]{2,0,1,3:T(2,128)(2,1)}, u32[]{:S(2)}, u32[]{:S(2)}) async-start(bf16[2,1,192,1536]{2,0,1,3:T(2,128)(2,1)} %copy.189), calls=%async_computation | async-start | bytes 3145728 | tf_op jit(solution)/shard_map/all_to_all | solution.py:83
  36.0 40.8 %all-to-all-start.1 = ((bf16[4,2,36864]{2,1,0:T(2,128)(2,1)}), bf16[4,2,36864]{2,1,0:T(2,128)(2,1)}, u32[]{:S(2)}, u32[]{:S(2)}) async-start(bf16[4,2,36864]{2,1,0:T(2,128)(2,1)} %reshape.571), calls=%async_computation.1 | async-start | bytes 1179648 | tf_op jit(solution)/shard_map/all_to_all | solution.py:82
  41.5 364.4 %all-reduce.3.cloned.1.call-start = ((), (), s32[]{:S(2)}) async-start(), calls=%async_computation.5 | async-start | bytes 9437184 | tf_op jit(solution)/shard_map/psum | solution.py:72
  47.0 39.6 %collective-permute-start.1 = (bf16[2,1,768,384]{3,2,0,1:T(8,128)(2,1)}, bf16[2,1,768,384]{3,2,0,1:T(8,128)(2,1)}, u32[]{:S(2)}, u32[]{:S(2)}) collective-permute-start(bf16[2,1,768,384]{3,2,0,1:T(8,128)(2,1)} %bitcast.7), channel_id=1, source_target_pairs={{4,0},{8,4},{12,8},{5,1},{9,5},{13,9},{6,2},{10,6},{14,10},{7,3},{... | collective-permute-start | bytes 3538952 | tf_op jit(solution)/shard_map/ppermute | solution.py:21
  48.3 39.9 %collective-permute-start = (bf16[2,1,768,384]{3,2,0,1:T(8,128)(2,1)}, bf16[2,1,768,384]{3,2,0,1:T(8,128)(2,1)}, u32[]{:S(2)}, u32[]{:S(2)}) collective-permute-start(bf16[2,1,768,384]{3,2,0,1:T(8,128)(2,1)} %bitcast.7), channel_id=1, source_target_pairs={{0,4},{4,8},{8,12},{1,5},{5,9},{9,13},{2,6},{6,10},{10,14},{3,7},{... | collective-permute-start | bytes 3538952 | tf_op jit(solution)/shard_map/ppermute | solution.py:20
  63.8 6.8 %copy-start.51 = (s32[5]{0:T(128)S(1)}, s32[5]{0:T(128)}, u32[]{:S(2)}) copy-start(s32[5]{0:T(128)} %constant.262.clone.1) | copy-start | bytes 64
  67.9 8.8 %copy-start.48 = (s32[2]{0:T(128)}, s32[2]{0:T(128)S(1)}, u32[]{:S(2)}) copy-start(s32[2]{0:T(128)S(1)} %iota.33) | copy-start | bytes 28
  91.8 8.5 %copy-start.7 = (pred[768,2304]{0,1:T(32,128)(4,1)S(1)}, pred[768,2304]{0,1:T(32,128)(4,1)}, u32[]{:S(2)}) copy-start(pred[768,2304]{0,1:T(32,128)(4,1)} %copy.201) | copy-start | bytes 5308420
  110.2 5.1 %copy-start.9 = (pred[768,2304]{0,1:T(32,128)(4,1)S(1)}, pred[768,2304]{0,1:T(32,128)(4,1)}, u32[]{:S(2)}) copy-start(pred[768,2304]{0,1:T(32,128)(4,1)} %copy.211) | copy-start | bytes 5308420
  117.6 6.7 %copy-start.5 = (f32[2304,768]{1,0:T(8,128)}, f32[2304,768]{1,0:T(8,128)S(1)}, u32[]{:S(2)}) copy-start(f32[2304,768]{1,0:T(8,128)S(1)} %get-tuple-element.140) | copy-start | bytes 21233668
  135.0 5.4 %copy-start.4 = (f32[2304,768]{1,0:T(8,128)}, f32[2304,768]{1,0:T(8,128)S(1)}, u32[]{:S(2)}) copy-start(f32[2304,768]{1,0:T(8,128)S(1)} %get-tuple-element.142) | copy-start | bytes 21233668
  136.9 6.6 %slice-start = ((s8[7077888]{0:T(1024)(128)(4,1)}), s8[4194304]{0:T(1024)(128)(4,1)S(1)}, s32[]{:S(2)}) async-start(s8[7077888]{0:T(1024)(128)(4,1)} %bitcast.294), calls=%async_computation.6 | async-start | bytes 8388608
  140.5 6.9 %slice-start.2 = ((s8[7077888]{0:T(1024)(128)(4,1)}), s8[2883584]{0:T(1024)(128)(4,1)S(1)}, s32[]{:S(2)}) async-start(s8[7077888]{0:T(1024)(128)(4,1)} %bitcast.296), calls=%async_computation.8 | async-start | bytes 5767168
  150.4 5.5 %copy-start.13 = (bf16[768,2304]{0,1:T(8,128)(2,1)}, bf16[768,2304]{0,1:T(8,128)(2,1)S(1)}, u32[]{:S(2)}) copy-start(bf16[768,2304]{0,1:T(8,128)(2,1)S(1)} %multiply_convert_fusion) | copy-start | bytes 10616836
  160.7 10.8 %copy-start.45 = (f32[768]{0:T(1024)S(1)}, f32[768]{0:T(1024)}, u32[]{:S(2)}) copy-start(f32[768]{0:T(1024)} %copy-done.44) | copy-start | bytes 9220
  160.7 10.8 %copy-start.53 = (f32[768]{0:T(1024)S(1)}, f32[768]{0:T(1024)}, u32[]{:S(2)}) copy-start(f32[768]{0:T(1024)} %get-tuple-element.102) | copy-start | bytes 9220
  164.9 6.5 %copy-start.34 = (bf16[1,3,768,1,128]{4,2,1,3,0:T(8,128)(2,1)S(1)}, bf16[1,3,768,1,128]{4,2,1,3,0:T(8,128)(2,1)}, u32[]{:S(2)}) copy-start(bf16[1,3,768,1,128]{4,2,1,3,0:T(8,128)(2,1)} %copy.207) | copy-start | bytes 1769476
  171.5 7.0 %copy-start.18 = (bf16[1,768,1,128]{3,2,1,0:T(2,128)(2,1)S(1)}, bf16[1,768,1,128]{3,2,1,0:T(2,128)(2,1)}, u32[]{:S(2)}) copy-start(bf16[1,768,1,128]{3,2,1,0:T(2,128)(2,1)} %get-tuple-element.115) | copy-start | bytes 589828
  188.8 11.8 %slice-start.4 = ((s8[4718592]{0:T(1024)(128)(4,1)}), s8[4194304]{0:T(1024)(128)(4,1)S(1)}, s32[]{:S(2)}) async-start(s8[4718592]{0:T(1024)(128)(4,1)} %bitcast.353), calls=%async_computation.10 | async-start | bytes 8388608
  191.5 9.1 %slice-start.5 = ((s8[4718592]{0:T(1024)(128)(4,1)}), s8[524288]{0:T(1024)(128)(4,1)S(1)}, s32[]{:S(2)}) async-start(s8[4718592]{0:T(1024)(128)(4,1)} %bitcast.353), calls=%async_computation.11 | async-start | bytes 1048576
  194.3 6.2 %copy-start.40 = (bf16[768,128]{0,1:T(8,128)(2,1)S(1)}, bf16[768,128]{0,1:T(8,128)(2,1)}, u32[]{:S(2)}) copy-start(bf16[768,128]{0,1:T(8,128)(2,1)} %fusion.48) | copy-start | bytes 589828
  194.3 6.2 %copy-start.42 = (bf16[768,128]{0,1:T(8,128)(2,1)S(1)}, bf16[768,128]{0,1:T(8,128)(2,1)}, u32[]{:S(2)}) copy-start(bf16[768,128]{0,1:T(8,128)(2,1)} %copy-done.41) | copy-start | bytes 589828
  194.3 6.2 %copy-start.43 = (bf16[768,128]{0,1:T(8,128)(2,1)S(1)}, bf16[768,128]{0,1:T(8,128)(2,1)}, u32[]{:S(2)}) copy-start(bf16[768,128]{0,1:T(8,128)(2,1)} %get-tuple-element.143) | copy-start | bytes 589828
  195.9 25.5 %collective-permute-start.2 = (bf16[1,2,768,3,128]{2,4,3,1,0:T(8,128)(2,1)}, bf16[1,2,768,3,128]{2,4,3,1,0:T(8,128)(2,1)}, u32[]{:S(2)}, u32[]{:S(2)}) collective-permute-start(bf16[1,2,768,3,128]{2,4,3,1,0:T(8,128)(2,1)} %get-tuple-element.105), channel_id=1, source_target_pairs={{0,4},{4,8},{8,12},{1,5},{5,9},{9,13},{2,6},{6,10},{10,14},{3,7},{... | collective-permute-start | bytes 3538952 | tf_op jit(solution)/shard_map/ppermute | solution.py:20
  199.2 22.2 %collective-permute-start.3 = (bf16[1,2,768,3,128]{2,4,3,1,0:T(8,128)(2,1)}, bf16[1,2,768,3,128]{2,4,3,1,0:T(8,128)(2,1)}, u32[]{:S(2)}, u32[]{:S(2)}) collective-permute-start(bf16[1,2,768,3,128]{2,4,3,1,0:T(8,128)(2,1)} %get-tuple-element.106), channel_id=1, source_target_pairs={{4,0},{8,4},{12,8},{5,1},{9,5},{13,9},{6,2},{10,6},{14,10},{7,3},{... | collective-permute-start | bytes 3538952 | tf_op jit(solution)/shard_map/ppermute | solution.py:21
  216.6 14.9 %all-to-all-start.2 = ((bf16[4,2,36864]{2,1,0:T(2,128)(2,1)}), bf16[4,2,36864]{2,1,0:T(2,128)(2,1)S(1)}, u32[]{:S(2)}, u32[]{:S(2)}) async-start(bf16[4,2,36864]{2,1,0:T(2,128)(2,1)} %reshape.573), calls=%async_computation.2 | async-start | bytes 1179648 | tf_op jit(solution)/shard_map/all_to_all | solution.py:157
  231.4 14.4 %all-to-all-start.3 = ((bf16[4,2,36864]{2,1,0:T(2,128)(2,1)}), bf16[4,2,36864]{2,1,0:T(2,128)(2,1)S(1)}, u32[]{:S(2)}, u32[]{:S(2)}) async-start(bf16[4,2,36864]{2,1,0:T(2,128)(2,1)} %reshape.575), calls=%async_computation.3 | async-start | bytes 1179648 | tf_op jit(solution)/shard_map/all_to_all | solution.py:158
  245.8 13.3 %all-to-all-start.4 = ((bf16[4,2,36864]{2,1,0:T(2,128)(2,1)}), bf16[4,2,36864]{2,1,0:T(2,128)(2,1)S(1)}, u32[]{:S(2)}, u32[]{:S(2)}) async-start(bf16[4,2,36864]{2,1,0:T(2,128)(2,1)} %reshape.577), calls=%async_computation.4 | async-start | bytes 1179648 | tf_op jit(solution)/shard_map/all_to_all | solution.py:159
  259.7 150.3 %copy-start.1 = (bf16[384,3072]{1,0:T(8,128)(2,1)S(1)}, bf16[384,3072]{1,0:T(8,128)(2,1)}, u32[]{:S(2)}) copy-start(bf16[384,3072]{1,0:T(8,128)(2,1)} %param.27) | copy-start | bytes 7077892
  (38 other events, 111.2 us)
Sparse Core Ops, SparseCore 0:
  204.9 200.9 all-reduce.2
where the time goes:
time: 423 us; the launch traced here: 417 us
  waiting for transfers between devices  156 us (37%)
  local copies, waits for them, and re-layouts  102 us (24%)
  matrix products  62 us (15%)
  other arithmetic  43.7 us (10%)
  starting transfers between devices  37.5 us (9%)
  between operations  15.5 us (4%)
    psum x1, waiting for transfers between devices, weight_sum(): grand_total = lax.psum(local_term, ('dp', 'ctx'))  145 us
    unnamed x7, other arithmetic  22.5 us
    unnamed x135, local copies, waits for them, and re-layouts  19 us
    slice x12, local copies, waits for them, and re-layouts, cross_rounded(): return jnp.concatenate([lowered[0:1], parts[1:2], lowered[2:3]], axis=0)  14.2 us
    dot_general x3, matrix products, backward_block(): lax.dot_general(mixing_low, grad_tile, (((0,), (0,)), ((), ())), preferre...  12.9 us
    broadcast_in_dim x7, local copies, waits for them, and re-layouts, forward_block(): raised = jnp.where(key_mask, jnp.exp(score_grid - row_max), 0.0)  11.7 us
    dot_general x3, matrix products, backward_block(): jnp.dot(grad_tile, value_window.T, preferred_element_type=jnp.float32)  11 us
    dot_general x3, matrix products, forward_block(): jnp.dot(mixing.astype(jnp.bfloat16), value_window, preferred_element_type...  9.95 us
  transfers between devices with their start and end apart: 10, of which 5 were waited for; matrix products, arithmetic and copies ran while one was open for 22% of the time, Pallas kernels for 0%

commit v1 on v0

--- a/solution.py
+++ b/solution.py
@@ -69,8 +69,11 @@
     local_term = lax.dot_general(
         attended, token_grads, (((0,), (0,)), ((), ())), preferred_element_type=jnp.float32
     )
-    grand_total = lax.psum(local_term, ("dp", "ctx"))
-    return (grand_total / lax.axis_size("dp")).astype(jnp.bfloat16)
+    rows, cols = local_term.shape
+    part = lax.psum_scatter(local_term, ("dp", "ctx"), scatter_dimension=1, tiled=True)
+    part = (part / lax.axis_size("dp")).astype(jnp.bfloat16)
+    whole = lax.all_gather(part, ("dp", "ctx"), axis=1, tiled=True)
+    return whole.reshape(rows, cols)
 
 
 def on_device(queries, key_rows, value_rows, out_grad, out_weight, tile_lists, windows):
@@ -136,15 +139,19 @@
         return pair_total
 
     frame_at = 0
+    saved = []
     for head_at in range(heads_here):
         query_tile, key_window, value_window = tiles_of(frame_at, head_at)
         mixing, out_low, row_max, totals = forward_block(
             query_tile, key_window, value_window, allowed[frame_at, head_at]
         )
         out_blocks[frame_at][head_at] = out_low
-        pair_total = add_back(pair_total, frame_at, head_at, mixing, out_low)
+        saved.append((mixing, out_low))
     attended = assemble(out_blocks)
     weight_grad = weight_sum(attended, out_grad[0])
+    for head_at in range(heads_here):
+        mixing, out_low = saved[head_at]
+        pair_total = add_back(pair_total, frame_at, head_at, mixing, out_low)
     outgoing = jnp.stack([pair_total[:, 0], pair_total[:, FT_DEV + 1]]).astype(jnp.bfloat16)
     returned = extended(outgoing, (("ctx", 0),), 1).astype(jnp.float32)
     own_grads = pair_total[:, 1 : FT_DEV + 1]

time: 423 us -> 538 us (1.27)
  waiting for transfers between devices: 156 us -> 235 us
  local copies, waits for them, and re-layouts: 102 us -> 117 us
  other arithmetic: 43.7 us -> 53.9 us
  matrix products: 62 us -> 72 us
    reduce_scatter x0 -> x1, waiting for transfers between devices: none -> 195 us  [weight_sum(): lax.psum_scatter(local_term, ('dp', 'ctx'), scatter_dimension=1, tiled=True)]
    psum x1 -> x0, waiting for transfers between devices: 145 us -> none  [weight_sum(): grand_total = lax.psum(local_term, ('dp', 'ctx'))]
    all_gather x0 -> x1, waiting for transfers between devices: none -> 29 us  [weight_sum(): whole = lax.all_gather(part, ('dp', 'ctx'), axis=1, tiled=True)]
    unnamed x135 -> x114, local copies, waits for them, and re-layouts: 19 us -> 28.5 us
    dot_general x3, matrix products: 11 us -> 19.6 us  [backward_block(): jnp.dot(grad_tile, value_window.T, preferred_element_type=jnp.float32)]
    dot_general x3, matrix products: 12.9 us -> 18.4 us  [backward_block(): lax.dot_general(mixing_low, grad_tile, (((0,), (0,)), ((), ())), preferre...]
    unnamed x7 -> x6, other arithmetic: 22.5 us -> 22.3 us
  transfers between devices with their start and end apart: 10 -> 11, of which waited for: 5 -> 6; matrix products, arithmetic and copies ran while one was open for 22% -> 34% of each run, Pallas kernels for 0% -> 0%
where the time goes in v1:
time: 538 us; the launch traced here: 531 us
  waiting for transfers between devices  235 us (44%)
  local copies, waits for them, and re-layouts  117 us (22%)
  matrix products  72 us (13%)
  other arithmetic  53.9 us (10%)
  starting transfers between devices  37.8 us (7%)
  between operations  15.1 us (3%)
    reduce_scatter x1, waiting for transfers between devices, weight_sum(): lax.psum_scatter(local_term, ('dp', 'ctx'), scatter_dimension=1, tiled=True)  195 us
    all_gather x1, waiting for transfers between devices, weight_sum(): whole = lax.all_gather(part, ('dp', 'ctx'), axis=1, tiled=True)  29 us
    unnamed x114, local copies, waits for them, and re-layouts  28.5 us
    unnamed x6, other arithmetic  22.3 us
    dot_general x3, matrix products, backward_block(): jnp.dot(grad_tile, value_window.T, preferred_element_type=jnp.float32)  19.6 us
    dot_general x3, matrix products, backward_block(): lax.dot_general(mixing_low, grad_tile, (((0,), (0,)), ((), ())), preferre...  18.4 us
    broadcast_in_dim x7, local copies, waits for them, and re-layouts, forward_block(): raised = jnp.where(key_mask, jnp.exp(score_grid - row_max), 0.0)  11.6 us
  transfers between devices with their start and end apart: 11, of which 6 were waited for; matrix products, arithmetic and copies ran while one was open for 34% of the time, Pallas kernels for 0%

profile of v1, /device:TPU:2, one launch (start us, length us, event | category | flops | bytes accessed | tf_op | source)
XLA Modules:
  0.0 530.6 jit_solution(8321578689690815103)
XLA Ops:
  8.7 2.9 copy.194
  11.6 6.7 %all-to-all-start = ((bf16[2,1,192,1536]{2,0,1,3:T(2,128)(2,1)}), bf16[2,1,192,1536]{2,0,1,3:T(2,128)(2,1)}, u32[]{:S(2)}, u32[]{:S(2)}) async-start(bf16[2,1,192,1536]{2,0,1,3:T(2,128)(2,1)} %copy.194), calls=%async_computation | async-start | bytes 3145728 | tf_op jit(solution)/shard_map/all_to_all | solution.py:86
  21.7 9.8 %reduce.34 = bf16[1536,192]{1,0:T(8,128)(2,1)S(1)} reduce(bf16[1536,1,1,192]{3,2,1,0:T(2,128)(2,1)} %bitcast.302, bf16[]{:T(256)} %broadcast.396), dimensions={1,2}, to_apply=%bitcast.238.reduce_sub_computation | reduce | bytes 1179650
  36.0 5.5 %all-to-all-start.1 = ((bf16[4,2,36864]{2,1,0:T(2,128)(2,1)}), bf16[4,2,36864]{2,1,0:T(2,128)(2,1)}, u32[]{:S(2)}, u32[]{:S(2)}) async-start(bf16[4,2,36864]{2,1,0:T(2,128)(2,1)} %reshape.571), calls=%async_computation.1 | async-start | bytes 1179648 | tf_op jit(solution)/shard_map/all_to_all | solution.py:85
  41.5 4.3 copy.243
  48.4 4.3 collective-permute-start
  54.8 3.2 copy.211
  59.6 3.2 copy.216
  64.4 3.2 copy.206
  70.9 5.4 %fusion.34 = bf16[768,384]{0,1:T(8,128)(2,1)} fusion(bf16[384,3072]{1,0:T(8,128)(2,1)S(1)} %copy-done, bf16[1,768,3072]{2,1,0:T(8,128)(2,1)} %param.26), kind=kOutput, calls=%fused_computation.49 | convolution fusion | flops 1812234240 | bytes 7667712 | tf_op jit(solution)/shard_map/dot_general | solution.py:93
  105.2 4.9 fusion.92
  129.1 3.2 multiply_reduce_fusion.2
  132.3 4.4 fusion.9
  137.0 6.9 %fusion.96 = (bf16[2304,128]{0,1:T(8,128)(2,1)S(1)}, f32[2304,128]{0,1:T(8,128)}) fusion(bf16[1,768,3,128]{1,3,2,0:T(8,128)(2,1)} %bitcast.354, f32[768]{0:T(1024)} %copy-done.35, pred[768,2304]{0,1:T(32,128)(4,1)} %copy.216, f32[768]{0:T(1024)S(1)} %get-tuple-element.163, f32[2304,768]{1,0:T(8,128)} %copy-done.3), kind=kOutput, calls=%fused_computation.147 | convolution fusion | flops 462127104 | bytes 10820608 | tf_op jit(solution)/shard_map/dot_general | solution.py:56
  146.4 6.6 %multiply_convert_fusion.2 = bf16[768,2304]{0,1:T(8,128)(2,1)S(1)} fusion(bf16[2304,128]{1,0:T(8,128)(2,1)} %bitcast.337, f32[768]{0:T(1024)} %get-tuple-element.124, bf16[1,768,3,128]{1,3,2,0:T(8,128)(2,1)} %bitcast.355, f32[768]{0:T(1024)} %copy-done.37, pred[768,2304]{0,1:T(32,128)(4,1)} %copy.206, f32[768]{0:T(1024)S(1)} %get-tuple-element.161, ...), kind=kOutput, calls=%fused_computation.17 | convolution fusion | flops 467140608 | bytes 13184000 | tf_op jit(solution)/shard_map/dot_general | solution.py:59
  161.5 6.6 %multiply_convert_fusion = bf16[768,2304]{0,1:T(8,128)(2,1)S(1)} fusion(bf16[2304,128]{1,0:T(8,128)(2,1)} %bitcast.335, f32[768]{0:T(1024)} %get-tuple-element.125, bf16[1,768,3,128]{1,3,2,0:T(8,128)(2,1)} %bitcast.356, f32[768]{0:T(1024)S(1)} %copy-done.36, pred[768,2304]{0,1:T(32,128)(4,1)} %copy.216, f32[768]{0:T(1024)S(1)} %get-tuple-element.163, ...), kind=kOutput, calls=%fused_computation.15 | convolution fusion | flops 467140608 | bytes 13182976 | tf_op jit(solution)/shard_map/dot_general | solution.py:59
  176.7 6.3 %multiply_convert_fusion.1 = bf16[768,2304]{0,1:T(8,128)(2,1)S(1)} fusion(bf16[2304,128]{1,0:T(8,128)(2,1)} %bitcast.333, f32[768]{0:T(1024)S(1)} %copy-done.44, bf16[1,768,3,128]{1,3,2,0:T(8,128)(2,1)} %bitcast.357, f32[768]{0:T(1024)S(1)} %fusion.16, pred[768,2304]{0,1:T(32,128)(4,1)S(1)} %copy-done.5, f32[768]{0:T(1024)S(1)} %get-tuple-element.165, ...), kind=kOutput, calls=%fused_computation.16 | convolution fusion | flops 467140608 | bytes 13181952 | tf_op jit(solution)/shard_map/dot_general | solution.py:59
  191.7 6.6 %fusion.94 = (bf16[2304,128]{0,1:T(8,128)(2,1)}, f32[2304,128]{0,1:T(8,128)}) fusion(bf16[1,768,3,128]{1,3,2,0:T(8,128)(2,1)} %bitcast.358, f32[768]{0:T(1024)S(1)} %fusion.16, pred[768,2304]{0,1:T(32,128)(4,1)S(1)} %copy-done.5, f32[768]{0:T(1024)S(1)} %get-tuple-element.165, f32[2304,768]{1,0:T(8,128)} %copy-done.2), kind=kOutput, calls=%fused_computation.145 | convolution fusion | flops 462127104 | bytes 10819584 | tf_op jit(solution)/shard_map/dot_general | solution.py:56
  202.0 3.5 scatter-add.20
  215.0 194.7 %reduce-scatter.2.cloned.1.call-done = f32[384,48]{0,1:T(8,128)} async-done(((f32[384,3072]{0,1:T(8,128)}), f32[384,48]{0,1:T(8,128)}) %reduce-scatter.2.cloned.1.call-update) | async-done | bytes 73744 | tf_op jit(solution)/shard_map/reduce_scatter | solution.py:73
  411.2 4.1 fusion.37
  417.9 4.2 fusion.38
  425.7 3.7 convert.12
  438.9 4.2 reduce.35
  444.0 4.8 all-to-all-start.2
  452.8 4.2 reduce.36
  458.8 5.1 all-to-all-start.3
  465.2 4.2 reduce.37
  473.1 5.6 %all-to-all-start.4 = ((bf16[4,2,36864]{2,1,0:T(2,128)(2,1)}), bf16[4,2,36864]{2,1,0:T(2,128)(2,1)}, u32[]{:S(2)}, u32[]{:S(2)}) async-start(bf16[4,2,36864]{2,1,0:T(2,128)(2,1)} %reshape.577), calls=%async_computation.4 | async-start | bytes 1179648 | tf_op jit(solution)/shard_map/all_to_all | solution.py:166
  481.7 5.3 %all-to-all-done.4 = bf16[4,2,36864]{2,1,0:T(2,128)(2,1)} async-done(((bf16[4,2,36864]{2,1,0:T(2,128)(2,1)}), bf16[4,2,36864]{2,1,0:T(2,128)(2,1)}, u32[]{:S(2)}, u32[]{:S(2)}) %all-to-all-start.4) | async-done | bytes 589856 | tf_op jit(solution)/shard_map/all_to_all | solution.py:166
  490.3 29.0 %all-gather.2.cloned.1.call-done = bf16[384,3072]{0,1:T(8,128)(2,1)} async-done(((bf16[384,48]{0,1:T(8,128)(2,1)}), bf16[384,3072]{0,1:T(8,128)(2,1)}) %all-gather.2.cloned.1.call-update) | async-done | bytes 2359312 | tf_op jit(solution)/shard_map/all_gather | solution.py:75
  519.3 4.3 copy.239
  (223 shorter events, 144.7 us)
Async XLA Ops:
  7.2 63.7 %copy-start = (bf16[384,3072]{1,0:T(8,128)(2,1)S(1)}, bf16[384,3072]{1,0:T(8,128)(2,1)}, u32[]{:S(2)}) copy-start(bf16[384,3072]{1,0:T(8,128)(2,1)} %param.27) | copy-start | bytes 7077892
  8.7 9.6 %copy-start.41 = (s32[12,2]{0,1:T(2,128)S(1)}, s32[12,2]{0,1:T(2,128)}, u32[]{:S(2)}) copy-start(s32[12,2]{0,1:T(2,128)} %param.29) | copy-start | bytes 292
  11.6 6.8 %copy-start.34 = (bf16[1,192,1536]{2,1,0:T(8,128)(2,1)S(1)}, bf16[1,192,1536]{2,1,0:T(8,128)(2,1)}, u32[]{:S(2)}) copy-start(bf16[1,192,1536]{2,1,0:T(8,128)(2,1)} %param.23) | copy-start | bytes 1769476
  11.6 24.5 %all-to-all-start = ((bf16[2,1,192,1536]{2,0,1,3:T(2,128)(2,1)}), bf16[2,1,192,1536]{2,0,1,3:T(2,128)(2,1)}, u32[]{:S(2)}, u32[]{:S(2)}) async-start(bf16[2,1,192,1536]{2,0,1,3:T(2,128)(2,1)} %copy.194), calls=%async_computation | async-start | bytes 3145728 | tf_op jit(solution)/shard_map/all_to_all | solution.py:86
  36.0 40.3 %all-to-all-start.1 = ((bf16[4,2,36864]{2,1,0:T(2,128)(2,1)}), bf16[4,2,36864]{2,1,0:T(2,128)(2,1)}, u32[]{:S(2)}, u32[]{:S(2)}) async-start(bf16[4,2,36864]{2,1,0:T(2,128)(2,1)} %reshape.571), calls=%async_computation.1 | async-start | bytes 1179648 | tf_op jit(solution)/shard_map/all_to_all | solution.py:85
  41.5 368.1 %reduce-scatter.2.cloned.1.call-start = ((), (), s32[]{:S(2)}) async-start(), calls=%async_computation.6 | async-start | bytes 4792320 | tf_op jit(solution)/shard_map/reduce_scatter | solution.py:73
  47.1 39.1 %collective-permute-start.1 = (bf16[2,1,768,384]{3,2,0,1:T(8,128)(2,1)}, bf16[2,1,768,384]{3,2,0,1:T(8,128)(2,1)}, u32[]{:S(2)}, u32[]{:S(2)}) collective-permute-start(bf16[2,1,768,384]{3,2,0,1:T(8,128)(2,1)} %bitcast.7), channel_id=1, source_target_pairs={{4,0},{8,4},{12,8},{5,1},{9,5},{13,9},{6,2},{10,6},{14,10},{7,3},{... | collective-permute-start | bytes 3538952 | tf_op jit(solution)/shard_map/ppermute | solution.py:21
  48.4 39.4 %collective-permute-start = (bf16[2,1,768,384]{3,2,0,1:T(8,128)(2,1)}, bf16[2,1,768,384]{3,2,0,1:T(8,128)(2,1)}, u32[]{:S(2)}, u32[]{:S(2)}) collective-permute-start(bf16[2,1,768,384]{3,2,0,1:T(8,128)(2,1)} %bitcast.7), channel_id=1, source_target_pairs={{0,4},{4,8},{8,12},{1,5},{5,9},{9,13},{2,6},{6,10},{10,14},{3,7},{... | collective-permute-start | bytes 3538952 | tf_op jit(solution)/shard_map/ppermute | solution.py:20
  63.5 6.7 %copy-start.42 = (s32[5]{0:T(128)S(1)}, s32[5]{0:T(128)}, u32[]{:S(2)}) copy-start(s32[5]{0:T(128)} %constant.262.clone.1) | copy-start | bytes 64
  67.6 8.7 %copy-start.39 = (s32[2]{0:T(128)}, s32[2]{0:T(128)S(1)}, u32[]{:S(2)}) copy-start(s32[2]{0:T(128)S(1)} %iota.33) | copy-start | bytes 28
  91.3 8.5 %copy-start.8 = (pred[768,2304]{0,1:T(32,128)(4,1)S(1)}, pred[768,2304]{0,1:T(32,128)(4,1)}, u32[]{:S(2)}) copy-start(pred[768,2304]{0,1:T(32,128)(4,1)} %copy.206) | copy-start | bytes 5308420
  136.8 382.5 %all-gather.2.cloned.1.call-start = ((), (), s32[]{:S(2)}) async-start(), calls=%async_computation.7 | async-start | bytes 2396160 | tf_op jit(solution)/shard_map/all_gather | solution.py:75
  146.3 8.4 %copy-start.26 = (bf16[1,768,1,128]{3,2,1,0:T(2,128)(2,1)S(1)}, bf16[1,768,1,128]{3,2,1,0:T(2,128)(2,1)}, u32[]{:S(2)}) copy-start(bf16[1,768,1,128]{3,2,1,0:T(2,128)(2,1)} %get-tuple-element.141) | copy-start | bytes 589828
  154.8 6.8 %copy-start.36 = (f32[768]{0:T(1024)S(1)}, f32[768]{0:T(1024)}, u32[]{:S(2)}) copy-start(f32[768]{0:T(1024)} %copy-done.35) | copy-start | bytes 9220
  161.5 8.4 %copy-start.25 = (bf16[1,768,1,128]{3,2,1,0:T(2,128)(2,1)S(1)}, bf16[1,768,1,128]{3,2,1,0:T(2,128)(2,1)}, u32[]{:S(2)}) copy-start(bf16[1,768,1,128]{3,2,1,0:T(2,128)(2,1)} %get-tuple-element.140) | copy-start | bytes 589828
  170.0 6.8 %copy-start.44 = (f32[768]{0:T(1024)S(1)}, f32[768]{0:T(1024)}, u32[]{:S(2)}) copy-start(f32[768]{0:T(1024)} %get-tuple-element.126) | copy-start | bytes 9220
  176.7 8.2 %copy-start.24 = (bf16[1,768,1,128]{3,2,1,0:T(2,128)(2,1)S(1)}, bf16[1,768,1,128]{3,2,1,0:T(2,128)(2,1)}, u32[]{:S(2)}) copy-start(bf16[1,768,1,128]{3,2,1,0:T(2,128)(2,1)} %get-tuple-element.139) | copy-start | bytes 589828
  205.5 7.6 %copy-start.20 = (bf16[3,768,128]{1,2,0:T(8,128)(2,1)S(1)}, bf16[3,768,128]{1,2,0:T(8,128)(2,1)}, u32[]{:S(2)}) copy-start(bf16[3,768,128]{1,2,0:T(8,128)(2,1)} %copy.230) | copy-start | bytes 1769476
  206.7 7.4 %copy-start.21 = (bf16[3,768,128]{1,2,0:T(8,128)(2,1)S(1)}, bf16[3,768,128]{1,2,0:T(8,128)(2,1)}, u32[]{:S(2)}) copy-start(bf16[3,768,128]{1,2,0:T(8,128)(2,1)} %copy.226) | copy-start | bytes 1769476
  206.7 204.5 %copy-start.40 = (s32[2]{0:T(128)S(1)}, s32[2]{0:T(128)}, u32[]{:S(2)}) copy-start(s32[2]{0:T(128)} %copy-done.39) | copy-start | bytes 28
  213.1 202.3 %copy-start.19 = (bf16[3,768,128]{1,2,0:T(8,128)(2,1)S(1)}, bf16[3,768,128]{1,2,0:T(8,128)(2,1)}, u32[]{:S(2)}) copy-start(bf16[3,768,128]{1,2,0:T(8,128)(2,1)} %copy.228) | copy-start | bytes 1769476
  214.1 201.4 %copy-start.27 = (f32[1,768,128]{1,2,0:T(8,128)S(1)}, f32[1,768,128]{1,2,0:T(8,128)}, u32[]{:S(2)}) copy-start(f32[1,768,128]{1,2,0:T(8,128)} %slice_bitcast_fusion.5) | copy-start | bytes 1179652
  411.2 6.7 %copy-start.28 = (f32[1,768,128]{1,2,0:T(8,128)S(1)}, f32[1,768,128]{1,2,0:T(8,128)}, u32[]{:S(2)}) copy-start(f32[1,768,128]{1,2,0:T(8,128)} %slice_bitcast_fusion.4) | copy-start | bytes 1179652
  425.6 9.7 %copy-start.15 = (bf16[768,2304]{0,1:T(8,128)(2,1)S(1)}, bf16[768,2304]{0,1:T(8,128)(2,1)}, u32[]{:S(2)}) copy-start(bf16[768,2304]{0,1:T(8,128)(2,1)} %copy-done.14) | copy-start | bytes 10616836
  429.3 6.7 %copy-start.11 = (bf16[1,3,768,1,128]{4,2,1,3,0:T(8,128)(2,1)S(1)}, bf16[1,3,768,1,128]{4,2,1,3,0:T(8,128)(2,1)}, u32[]{:S(2)}) copy-start(bf16[1,3,768,1,128]{4,2,1,3,0:T(8,128)(2,1)} %copy-done.10) | copy-start | bytes 1769476
  429.3 6.7 %copy-start.13 = (bf16[768,2304]{0,1:T(8,128)(2,1)S(1)}, bf16[768,2304]{0,1:T(8,128)(2,1)}, u32[]{:S(2)}) copy-start(bf16[768,2304]{0,1:T(8,128)(2,1)} %copy-done.12) | copy-start | bytes 10616836
  430.9 17.9 %collective-permute-start.2 = (bf16[1,2,768,3,128]{2,4,3,1,0:T(8,128)(2,1)}, bf16[1,2,768,3,128]{2,4,3,1,0:T(8,128)(2,1)}, u32[]{:S(2)}, u32[]{:S(2)}) collective-permute-start(bf16[1,2,768,3,128]{2,4,3,1,0:T(8,128)(2,1)} %get-tuple-element.129), channel_id=1, source_target_pairs={{0,4},{4,8},{8,12},{1,5},{5,9},{9,13},{2,6},{6,10},{10,14},{3,7},{... | collective-permute-start | bytes 3538952 | tf_op jit(solution)/shard_map/ppermute | solution.py:20
  433.3 15.5 %collective-permute-start.3 = (bf16[1,2,768,3,128]{2,4,3,1,0:T(8,128)(2,1)}, bf16[1,2,768,3,128]{2,4,3,1,0:T(8,128)(2,1)}, u32[]{:S(2)}, u32[]{:S(2)}) collective-permute-start(bf16[1,2,768,3,128]{2,4,3,1,0:T(8,128)(2,1)} %get-tuple-element.130), channel_id=1, source_target_pairs={{4,0},{8,4},{12,8},{5,1},{9,5},{13,9},{6,2},{10,6},{14,10},{7,3},{... | collective-permute-start | bytes 3538952 | tf_op jit(solution)/shard_map/ppermute | solution.py:21
  444.0 14.8 %all-to-all-start.2 = ((bf16[4,2,36864]{2,1,0:T(2,128)(2,1)}), bf16[4,2,36864]{2,1,0:T(2,128)(2,1)S(1)}, u32[]{:S(2)}, u32[]{:S(2)}) async-start(bf16[4,2,36864]{2,1,0:T(2,128)(2,1)} %reshape.573), calls=%async_computation.2 | async-start | bytes 1179648 | tf_op jit(solution)/shard_map/all_to_all | solution.py:164
  458.8 14.2 %all-to-all-start.3 = ((bf16[4,2,36864]{2,1,0:T(2,128)(2,1)}), bf16[4,2,36864]{2,1,0:T(2,128)(2,1)S(1)}, u32[]{:S(2)}, u32[]{:S(2)}) async-start(bf16[4,2,36864]{2,1,0:T(2,128)(2,1)} %reshape.575), calls=%async_computation.3 | async-start | bytes 1179648 | tf_op jit(solution)/shard_map/all_to_all | solution.py:165
  473.1 14.0 %all-to-all-start.4 = ((bf16[4,2,36864]{2,1,0:T(2,128)(2,1)}), bf16[4,2,36864]{2,1,0:T(2,128)(2,1)}, u32[]{:S(2)}, u32[]{:S(2)}) async-start(bf16[4,2,36864]{2,1,0:T(2,128)(2,1)} %reshape.577), calls=%async_computation.4 | async-start | bytes 1179648 | tf_op jit(solution)/shard_map/all_to_all | solution.py:166
  489.3 34.2 %copy-start.1 = (bf16[384,3072]{1,0:T(8,128)(2,1)S(1)}, bf16[384,3072]{1,0:T(8,128)(2,1)}, u32[]{:S(2)}) copy-start(bf16[384,3072]{1,0:T(8,128)(2,1)} %param.27) | copy-start | bytes 7077892
  (28 other events, 100.7 us)
Sparse Core Ops, SparseCore 0:
  136.9 272.7 reduce-scatter.1
  411.5 107.7 all-gather.1
